TPU v7x, 32 devices: a whole 2x2x4 slice. The times are simulated.
32 devices in a mesh: dp: 8 (over z, y), ctx: 4 (over x, core).
Axes of the slice: x: 2, y: 2, z: 4, core: 2. Of those that a mesh axis runs over, the one named last changes fastest.
Arguments:
- queries: bfloat16 [4096, 4096], P(('dp', 'ctx')), may hold values from -40 to 40
- key_head_inputs: bfloat16 [4096, 512], P(('dp', 'ctx')), may hold values from -40 to 40
- value_head_inputs: bfloat16 [4096, 512], P(('dp', 'ctx')), may hold values from -6 to 6
- output_gradient: bfloat16 [4096, 4096], P(('dp', 'ctx')), may hold values from -6 to 6
- positions: int32 [4096], P(('dp', 'ctx')), may hold values from 0 to 1023, as said below
- counts: int32 [32], P(('dp', 'ctx')), may hold values from 64 to 128, as said below
- inputs: bfloat16 [4096, 8192], P(('dp', 'ctx')), may hold values from -6 to 6
Outputs:
- query_grad: bfloat16 [4096, 4096], P(('dp', 'ctx'))
- key_grad: bfloat16 [4096, 512], P(('dp', 'ctx'))
- value_grad: bfloat16 [4096, 512], P(('dp', 'ctx'))
- value_weight_gradient: float32 [512, 8192], P('dp', 'ctx')
Inputs may be any that keep to these rules, and one draw needn't show every extreme that they name: A device's valid slots are its first counts slots; the others are padding. Some device holds 128 valid slots. Along a sequence the positions of valid slots rise strictly; the first slot holds 0 and the last valid slot 1023. A padding slot repeats the position before it, or holds 1023 after the last valid slot.
All inputs are finite; a program needn't handle non-finite values.
Results may differ from a plain program's by a relative error of at most 0.0061.
Values may be sent and summed in bfloat16 or wider, within the bound.
No kernel may reach another device: no remote copies, remote signals or barrier semaphores. Data moves between devices by JAX's collectives and lax.ppermute only.
A program may use at most 128 MiB of HBM per device.

v0:
```python
import math
import jax
import jax.numpy as jnp
from jax import lax
from jax.sharding import PartitionSpec as P

HEAD_DIM = 128
QUERY_HEADS = 32
KEY_HEADS = 4
THETA = 500000.0


def rope_tables(position, head_size):
    half_width = head_size // 2
    frequency = jnp.exp(
        jnp.arange(half_width, dtype=jnp.float32) * (-2.0 * math.log(THETA) / head_size)
    )
    angles = position.astype(jnp.float32)[:, None] * frequency[None, :]
    return (jnp.cos(angles), jnp.sin(angles))


def apply_rotation(vectors, cosine_table, sine_lookup, sense):
    half_width = vectors.shape[-1] // 2
    lower_half = vectors[..., :half_width]
    upper_half = vectors[..., half_width:]
    cos_part = cosine_table[:, None, :]
    sin_part = sine_lookup[:, None, :] * sense
    return jnp.concatenate(
        [
            lower_half * cos_part - upper_half * sin_part,
            upper_half * cos_part + lower_half * sin_part,
        ],
        axis=-1,
    )


def per_device(
    queries, key_head_inputs, value_head_inputs, output_gradient, positions, counts, inputs
):
    row_number_total = queries.shape[0]
    query_group_width = QUERY_HEADS // KEY_HEADS
    axis_span = lax.axis_size("ctx")
    retained_slots = row_number_total * axis_span
    key_block = min(512, retained_slots)
    my_index = lax.axis_index("ctx")
    score_scale = 1.0 / math.sqrt(HEAD_DIM)
    cosine_table, sine_lookup = rope_tables(positions, HEAD_DIM)
    query_rotated = apply_rotation(
        queries.reshape(row_number_total, QUERY_HEADS, HEAD_DIM).astype(jnp.float32),
        cosine_table,
        sine_lookup,
        1.0,
    ).astype(jnp.bfloat16)
    key_rotated = apply_rotation(
        key_head_inputs.reshape(row_number_total, KEY_HEADS, HEAD_DIM).astype(jnp.float32),
        cosine_table,
        sine_lookup,
        1.0,
    ).astype(jnp.bfloat16)
    key_rotated = key_rotated.reshape(row_number_total, KEY_HEADS * HEAD_DIM)
    key_row_block, value_row_block, all_counts = (
        lax.all_gather(key_rotated, "ctx", axis=0, tiled=True),
        lax.all_gather(value_head_inputs, "ctx", axis=0, tiled=True),
        lax.all_gather(counts, "ctx", axis=0, tiled=True),
    )
    gathered_keys = key_row_block.reshape(retained_slots, KEY_HEADS, HEAD_DIM)
    gathered_values = value_row_block.reshape(retained_slots, KEY_HEADS, HEAD_DIM)
    key_valid = jnp.arange(retained_slots, dtype=jnp.int32) % row_number_total < jnp.repeat(
        all_counts, row_number_total
    )
    own_valid = jnp.arange(row_number_total, dtype=jnp.int32) < counts[0]
    initial_gradients = jnp.zeros((retained_slots, KEY_HEADS, HEAD_DIM), jnp.float32)
    first_slot = my_index * row_number_total
    key_accumulator = initial_gradients
    value_accumulator = initial_gradients
    query_count = query_rotated.shape[0]
    query_grouped = query_rotated.reshape(query_count, KEY_HEADS, query_group_width, HEAD_DIM)
    output_grad_grouped = output_gradient.reshape(
        query_count, KEY_HEADS, query_group_width, HEAD_DIM
    )
    q_slots = first_slot + jnp.arange(query_count, dtype=jnp.int32)
    block_total = (first_slot + query_count - 1) // key_block + 1

    def scores_for(begin_at):
        k_blk = lax.dynamic_slice_in_dim(gathered_keys, begin_at, key_block, 0)
        v_blk = lax.dynamic_slice_in_dim(gathered_values, begin_at, key_block, 0)
        k_slots = begin_at + jnp.arange(key_block, dtype=jnp.int32)
        k_valid = lax.dynamic_slice_in_dim(key_valid, begin_at, key_block, 0)
        allowed = own_valid[:, None] & k_valid[None, :] & (k_slots[None, :] <= q_slots[:, None])
        scores = (
            jnp.einsum("qhgd,khd->hgqk", query_grouped, k_blk, preferred_element_type=jnp.float32)
            * score_scale
        )
        d_probs = jnp.einsum(
            "qhgd,khd->hgqk", output_grad_grouped, v_blk, preferred_element_type=jnp.float32
        )
        return (k_blk, scores, d_probs, allowed)

    def first_pass(step_index, carry):
        row_top, row_total, weighted = carry
        k_blk, scores, d_probs, allowed = scores_for(step_index * key_block)
        new_top = jnp.maximum(row_top, jnp.max(jnp.where(allowed, scores, -1e30), axis=-1))
        factor = jnp.exp(row_top - new_top)
        exp_terms = jnp.where(allowed, jnp.exp(scores - new_top[..., None]), 0.0)
        return (
            new_top,
            row_total * factor + jnp.sum(exp_terms, axis=-1),
            weighted * factor + jnp.sum(exp_terms * d_probs, axis=-1),
        )

    statistic_shape = (KEY_HEADS, query_group_width, query_count)
    start_stats = (
        jnp.full(statistic_shape, -1e30, jnp.float32),
        jnp.zeros(statistic_shape, jnp.float32),
        jnp.zeros(statistic_shape, jnp.float32),
    )
    row_top, row_total, weighted = lax.fori_loop(0, block_total, first_pass, start_stats)
    row_total = jnp.where(own_valid[None, None, :], row_total, 1.0)
    row_delta = weighted / row_total

    def second_pass(step_index, carry):
        q_acc, key_sum, value_sum = carry
        begin_at = step_index * key_block
        k_blk, scores, d_probs, allowed = scores_for(begin_at)
        softmax = (
            jnp.where(allowed, jnp.exp(scores - row_top[..., None]), 0.0) / row_total[..., None]
        )
        d_scores = softmax * (d_probs - row_delta[..., None]) * score_scale
        prob_bf = softmax.astype(jnp.bfloat16)
        dscore_bf = d_scores.astype(jnp.bfloat16)
        q_acc = q_acc + jnp.einsum(
            "hgqk,khd->qhgd", dscore_bf, k_blk, preferred_element_type=jnp.float32
        )
        k_piece = jnp.einsum(
            "hgqk,qhgd->khd", dscore_bf, query_grouped, preferred_element_type=jnp.float32
        )
        v_piece = jnp.einsum(
            "hgqk,qhgd->khd", prob_bf, output_grad_grouped, preferred_element_type=jnp.float32
        )
        key_sum = lax.dynamic_update_slice_in_dim(
            key_sum,
            lax.dynamic_slice_in_dim(key_sum, begin_at, key_block, 0) + k_piece,
            begin_at,
            0,
        )
        value_sum = lax.dynamic_update_slice_in_dim(
            value_sum,
            lax.dynamic_slice_in_dim(value_sum, begin_at, key_block, 0) + v_piece,
            begin_at,
            0,
        )
        return (q_acc, key_sum, value_sum)

    query_offset = jnp.zeros((query_count, KEY_HEADS, query_group_width, HEAD_DIM), jnp.float32)
    q_acc, key_accumulator, value_accumulator = lax.fori_loop(
        0, block_total, second_pass, (query_offset, key_accumulator, value_accumulator)
    )
    q_grad_rot, key_accumulator, value_accumulator = (
        q_acc.reshape(query_count, QUERY_HEADS, HEAD_DIM),
        key_accumulator,
        value_accumulator,
    )
    key_portion, value_part = (
        lax.psum_scatter(
            key_accumulator.reshape(retained_slots, KEY_HEADS * HEAD_DIM),
            "ctx",
            scatter_dimension=0,
            tiled=True,
        ),
        lax.psum_scatter(
            value_accumulator.reshape(retained_slots, KEY_HEADS * HEAD_DIM),
            "ctx",
            scatter_dimension=0,
            tiled=True,
        ),
    )
    query_grad = (
        apply_rotation(q_grad_rot, cosine_table, sine_lookup, -1.0)
        .astype(jnp.bfloat16)
        .reshape(row_number_total, QUERY_HEADS * HEAD_DIM)
    )
    key_grad = (
        apply_rotation(
            key_portion.reshape(row_number_total, KEY_HEADS, HEAD_DIM),
            cosine_table,
            sine_lookup,
            -1.0,
        )
        .astype(jnp.bfloat16)
        .reshape(row_number_total, KEY_HEADS * HEAD_DIM)
    )
    value_grad = value_part.astype(jnp.bfloat16)
    weight_part = lax.psum_scatter(
        lax.dot_general(
            inputs, value_grad, (((0,), (0,)), ((), ())), preferred_element_type=jnp.float32
        ),
        "ctx",
        scatter_dimension=0,
        tiled=True,
    )
    shares = lax.psum_scatter(weight_part, "dp", scatter_dimension=1, tiled=True)
    return (query_grad, key_grad, value_grad, shares.T)


def solution(mesh):
    placed = (
        P(("dp", "ctx"), None),
        P(("dp", "ctx"), None),
        P(("dp", "ctx"), None),
        P(("dp", "ctx"), None),
        P(("dp", "ctx")),
        P(("dp", "ctx")),
        P(("dp", "ctx"), None),
    )
    return jax.shard_map(
        per_device,
        mesh=mesh,
        in_specs=placed,
        out_specs=(
            P(("dp", "ctx"), None),
            P(("dp", "ctx"), None),
            P(("dp", "ctx"), None),
            P("dp", "ctx"),
        ),
        check_vma=False,
    )
```

profile of v0, /device:TPU:0, one launch (start us, length us, event | category | flops | bytes accessed | tf_op | source)
XLA Modules:
  0.0 355.9 jit_solution(10259633255239488766)
XLA Ops:
  7.2 0.0 reduce-scatter.7.cloned.1.call-start
  8.1 1.2 dynamic-slice
  9.3 0.8 dynamic-update-slice
  10.1 0.7 convert_element_type.43
  10.7 6.4 %all-reduce = s32[4]{0:T(128)S(1)} all-reduce(s32[4]{0:T(128)S(1)} %dynamic-update-slice), channel_id=1, replica_groups=mesh['dp'=8,'ctx'=4] {'ctx'}, use_global_device_ids=true, to_apply=%add | all-reduce | flops 4 | bytes 32
  17.1 0.8 broadcast_multiply_fusion
  17.9 0.1 copy.20
  18.0 0.1 copy.21
  18.1 1.0 copy.24
  19.1 1.0 copy.46
  20.2 6.6 %all_gather.10 = bf16[512,512]{0,1:T(8,128)(2,1)S(1)} all-gather(bf16[128,512]{0,1:T(8,128)(2,1)S(1)} %bitcast.175), channel_id=1, replica_groups=mesh['dp'=8,'ctx'=4] {'ctx'}, dimensions={0}, use_global_device_ids=true | all-gather | bytes 655360 | tf_op jit(solution)/shard_map/all_gather | solution.py:62
  26.8 1.0 copy.29
  27.8 7.3 %all_gather.11 = bf16[512,512]{0,1:T(8,128)(2,1)S(1)} all-gather(bf16[128,512]{0,1:T(8,128)(2,1)S(1)} %copy.24), channel_id=1, replica_groups=mesh['dp'=8,'ctx'=4] {'ctx'}, dimensions={0}, use_global_device_ids=true | all-gather | bytes 655360 | tf_op jit(solution)/shard_map/all_gather | solution.py:63
  35.1 1.0 copy.27
  36.1 1.6 copy.25
  37.7 1.3 copy.28
  39.1 1.4 convert_bitcast_fusion
  40.5 0.4 copy.50
  40.9 0.8 subtract_convert_fusion.1
  41.7 0.4 copy.22
  42.1 0.4 copy.23
  42.5 0.6 pad_maximum_fusion
  43.1 7.6 %while.30 = (s32[]{:T(128)}, f32[4,8,128]{2,1,0:T(8,128)S(1)}, f32[4,8,128]{2,1,0:T(8,128)S(1)}, f32[4,8,128]{2,1,0:T(8,128)S(1)}, s32[]{:T(128)}, /*index=5*/bf...) while((s32[]{:T(128)}, f32[4,8,128]{2,1,0:T(8,128)S(1)}, ...), condition=%wide.region_4.5_spmd.clone, body=%wide.region_0.4_spmd.clone.sunk | while | flops 1099120896 | bytes 35166692 | solution.py:117
  43.2 0.1 fusion.84
  43.2 0.6 iota_compare_fusion.5
  43.9 0.2 compare_and_fusion.4
  44.1 2.3 fusion.85
  46.5 1.8 fusion.87
  48.3 2.4 fusion.86
  50.8 1.1 broadcast_in_dim.66.clone
  51.8 1.0 broadcast_in_dim.66
  52.9 1.6 broadcast_in_dim.50
  54.5 12.8 %while.31 = (s32[]{:T(128)}, f32[128,4,8,128]{3,0,2,1:T(8,128)}, f32[512,4,128]{2,0,1:T(8,128)}, f32[512,4,128]{2,0,1:T(8,128)}, s32[]{:T(128)}, /*index=5*/bf16...) while((s32[]{:T(128)}, f32[128,4,8,128]{3,0,2,1:T(8,128)}, ...), condition=%wide.region_6.7_spmd.clone, body=%wide.region_5.6_spmd.clone.sunk | while | flops 2704478464 | bytes 94034632 | solution.py:155
  54.5 0.1 fusion.98
  54.5 0.6 iota_compare_fusion.6
  55.2 0.2 compare_and_fusion.5
  55.4 3.4 fusion.99
  58.8 1.3 fusion.102
  60.2 1.3 fusion.100
  61.5 0.3 copy-done.6
  61.8 1.5 fusion.101
  63.3 0.1 copy-done.1
  63.4 0.1 copy-done.5
  63.5 2.4 bitcast_add_fusion.2
  65.9 1.4 copy-done.2
  67.2 2.3 copy_bitcast_fusion.1
  69.6 0.0 reduce-scatter.9.cloned.1.call-start
  69.6 25.8 %reduce-scatter.7.cloned.1.call-done = f32[128,512]{1,0:T(8,128)} async-done(((f32[512,512]{1,0:T(8,128)}), f32[128,512]{1,0:T(8,128)}) %reduce-scatter.7.cloned.1.call-update) | async-done | bytes 262160 | tf_op jit(solution)/shard_map/reduce_scatter | solution.py:170
  95.4 1.0 convert_element_type.49
  96.4 8.1 %convolution_bitcast_fusion.1 = f32[8192,512]{0,1:T(8,128)} fusion(bf16[128,512]{1,0:T(8,128)(2,1)S(1)} %convert_element_type.49, bf16[128,8192]{1,0:T(8,128)(2,1)S(1)} %copy-done), kind=kOutput, calls=%fused_computation.58 | convolution fusion | flops 1073741824 | bytes 19005440 | tf_op jit(solution)/shard_map/dot_general | solution.py:194
  104.6 0.0 reduce-scatter.5.cloned.1.call-start
  104.6 1.1 copy-done.8
  105.8 1.3 copy.35
  107.1 0.3 reduce-scatter.11.cloned.1.call-start
  107.4 122.3 %reduce-scatter.9.cloned.1.call-done = f32[2048,512]{0,1:T(8,128)} async-done(((f32[8192,512]{0,1:T(8,128)}), f32[2048,512]{0,1:T(8,128)}) %reduce-scatter.9.cloned.1.call-update) | async-done | bytes 4194320 | tf_op jit(solution)/shard_map/reduce_scatter | solution.py:193
  229.7 0.1 copy.34
  229.8 3.0 fusion.47
  232.8 2.7 subtract_convert_fusion
  235.5 0.6 pad_maximum_fusion.1
  236.1 1.4 copy.58
  237.5 19.5 %reduce-scatter.5.cloned.1.call-done = f32[128,512]{0,1:T(8,128)} async-done(((f32[512,512]{0,1:T(8,128)}), f32[128,512]{0,1:T(8,128)}) %reduce-scatter.5.cloned.1.call-update) | async-done | bytes 262160 | tf_op jit(solution)/shard_map/reduce_scatter | solution.py:164
  257.0 1.0 subtract_convert_fusion.2
  258.1 0.8 copy.45
  258.8 90.6 %reduce-scatter.11.cloned.1.call-done = f32[2048,64]{0,1:T(8,128)} async-done(((f32[2048,512]{0,1:T(8,128)}), f32[2048,64]{0,1:T(8,128)}) %reduce-scatter.11.cloned.1.call-update) | async-done | bytes 524304 | tf_op jit(solution)/shard_map/reduce_scatter | solution.py:201
  (54 shorter events, 0.3 us)
Async XLA Ops:
  7.2 89.2 %copy-start = (bf16[128,8192]{1,0:T(8,128)(2,1)S(1)}, bf16[128,8192]{1,0:T(8,128)(2,1)}, u32[]{:S(2)}) copy-start(bf16[128,8192]{1,0:T(8,128)(2,1)} %param.17) | copy-start | bytes 6291460
  7.2 88.3 %reduce-scatter.7.cloned.1.call-start = ((), (), s32[]{:S(2)}) async-start(), calls=%async_computation.5 | async-start | bytes 1310720 | tf_op jit(solution)/shard_map/reduce_scatter | solution.py:170
  17.9 2.3 copy-start.16
  18.0 22.9 %copy-start.13 = (f32[128,64]{1,0:T(8,128)}, f32[128,64]{1,0:T(8,128)S(1)}, u32[]{:S(2)}) copy-start(f32[128,64]{1,0:T(8,128)S(1)} %copy.20) | copy-start | bytes 98308
  46.5 1.8 copy-start.3
  46.5 1.8 copy-start.11
  55.4 3.4 copy-start.4
  55.4 3.4 copy-start.9
  58.8 1.3 copy-start.12
  60.2 1.3 copy-start.10
  60.2 1.6 copy-start.6
  61.8 1.6 copy-start.1
  61.8 1.7 copy-start.5
  63.5 2.4 copy-start.7
  65.9 1.4 copy-start.2
  69.6 160.1 %reduce-scatter.9.cloned.1.call-start = ((), (), s32[]{:S(2)}) async-start(), calls=%async_computation.6 | async-start | bytes 20971520 | tf_op jit(solution)/shard_map/reduce_scatter | solution.py:193
  96.4 8.1 %copy-start.15 = (bf16[128,512]{1,0:T(8,128)(2,1)}, bf16[128,512]{1,0:T(8,128)(2,1)S(1)}, u32[]{:S(2)}) copy-start(bf16[128,512]{1,0:T(8,128)(2,1)S(1)} %convert_element_type.49) | copy-start | bytes 393220
  104.5 1.2 copy-start.8
  104.6 125.1 %copy-start.18 = (f32[128,64]{0,1:T(8,128)S(1)}, f32[128,64]{0,1:T(8,128)}, u32[]{:S(2)}) copy-start(f32[128,64]{0,1:T(8,128)} %get-tuple-element.322) | copy-start | bytes 98308
  104.6 152.4 %reduce-scatter.5.cloned.1.call-start = ((), (), s32[]{:S(2)}) async-start(), calls=%async_computation.4 | async-start | bytes 1310720 | tf_op jit(solution)/shard_map/reduce_scatter | solution.py:164
  107.1 242.3 %reduce-scatter.11.cloned.1.call-start = ((), (), s32[]{:S(2)}) async-start(), calls=%async_computation.7 | async-start | bytes 4718592 | tf_op jit(solution)/shard_map/reduce_scatter | solution.py:201
  229.8 3.0 copy-start.14
  235.5 21.5 %copy-start.17 = (f32[128,64]{0,1:T(8,128)S(1)}, f32[128,64]{0,1:T(8,128)}, u32[]{:S(2)}) copy-start(f32[128,64]{0,1:T(8,128)} %copy-done.16) | copy-start | bytes 98308
Sparse Core Ops, SparseCore 0:
  69.7 25.6 reduce-scatter.6
  104.7 124.9 reduce-scatter.8
  232.2 24.7 reduce-scatter.4
  261.1 88.2 reduce-scatter.10
where the time goes:
time: 357 us; the launch traced here: 356 us
  waiting for transfers between devices  258 us (72%)
  local copies, waits for them, and re-layouts  26.1 us (7%)
  matrix products  22.7 us (6%)
  blocking collectives  20.3 us (6%)
  between operations  14.8 us (4%)
  other arithmetic  13.3 us (4%)
    reduce_scatter x1, waiting for transfers between devices, per_device(): lax.psum_scatter(lax.dot_general(inputs, value_grad, (((0,), (0,)), ((),...  122 us
    reduce_scatter x1, waiting for transfers between devices, per_device(): lax.psum_scatter(weight_part, 'dp', scatter_dimension=1, tiled=True)  90.6 us
    reduce_scatter x1, waiting for transfers between devices, per_device(): lax.psum_scatter(value_accumulator.reshape(retained_slots, KEY_HEADS * HE...  25.8 us
    reduce_scatter x1, waiting for transfers between devices, per_device(): lax.psum_scatter(key_accumulator.reshape(retained_slots, KEY_HEADS * HEAD...  19.5 us
    unnamed x26, local copies, waits for them, and re-layouts  10.9 us
    dot_general x1, matrix products, per_device(): lax.dot_general(inputs, value_grad, (((0,), (0,)), ((), ())), preferred_e...  8.12 us
    all_gather x1, blocking collectives, per_device(): lax.all_gather(value_head_inputs, 'ctx', axis=0, tiled=True)  7.29 us
  transfers between devices with their start and end apart: 4, of which 4 were waited for; matrix products, arithmetic and copies ran while one was open for 3% of the time, Pallas kernels for 0%

commit v1 on v0

--- a/solution.py
+++ b/solution.py
@@ -8,6 +8,22 @@
 QUERY_HEADS = 32
 KEY_HEADS = 4
 THETA = 500000.0
+
+
+def gather_around(x, axis, dim):
+    ways, here, turn = (lax.axis_size(axis), lax.axis_index(axis), x.shape[dim])
+    shape = [n * ways if d == dim else n for d, n in enumerate(x.shape)]
+    full = lax.dynamic_update_slice_in_dim(jnp.zeros(shape, x.dtype), x, here * turn, axis=dim)
+    going_up = going_down = x
+    for far in range(1, ways // 2 + 1):
+        going_up = lax.ppermute(going_up, axis, [(d, (d + 1) % ways) for d in range(ways)])
+        full = lax.dynamic_update_slice_in_dim(full, going_up, (here - far) % ways * turn, axis=dim)
+        if 2 * far < ways:
+            going_down = lax.ppermute(going_down, axis, [(d, (d - 1) % ways) for d in range(ways)])
+            full = lax.dynamic_update_slice_in_dim(
+                full, going_down, (here + far) % ways * turn, axis=dim
+            )
+    return full
 
 
 def rope_tables(position, head_size):
@@ -60,7 +76,7 @@
     key_rotated = key_rotated.reshape(row_number_total, KEY_HEADS * HEAD_DIM)
     key_row_block, value_row_block, all_counts = (
         lax.all_gather(key_rotated, "ctx", axis=0, tiled=True),
-        lax.all_gather(value_head_inputs, "ctx", axis=0, tiled=True),
+        gather_around(value_head_inputs, "ctx", 0),
         lax.all_gather(counts, "ctx", axis=0, tiled=True),
     )
     gathered_keys = key_row_block.reshape(retained_slots, KEY_HEADS, HEAD_DIM)

time: 357 us -> 364 us (1.020)
  local copies, waits for them, and re-layouts: 26.1 us -> 34.7 us
  blocking collectives: 20.3 us -> 12.8 us
    all_gather x1 -> x0, blocking collectives: 7.29 us -> none  [per_device(): lax.all_gather(value_head_inputs, 'ctx', axis=0, tiled=True)]
    unnamed x26 -> x28, local copies, waits for them, and re-layouts: 10.9 us -> 14.1 us
  transfers between devices with their start and end apart: 4 -> 7, of which waited for: 4 -> 5; matrix products, arithmetic and copies ran while one was open for 3% -> 9% of each run, Pallas kernels for 0% -> 0%
where the time goes in v1:
time: 364 us
  waiting for transfers between devices  261 us (72%)
  local copies, waits for them, and re-layouts  34.7 us (10%)
  matrix products  22.7 us (6%)
  other arithmetic  14.8 us (4%)
  between operations  14.7 us (4%)
  blocking collectives  12.8 us (4%)
    reduce_scatter x1, waiting for transfers between devices, per_device(): lax.psum_scatter(lax.dot_general(inputs, value_grad, (((0,), (0,)), ((),...  122 us
    reduce_scatter x1, waiting for transfers between devices, per_device(): lax.psum_scatter(weight_part, 'dp', scatter_dimension=1, tiled=True)  90.6 us
    reduce_scatter x1, waiting for transfers between devices, per_device(): lax.psum_scatter(value_accumulator.reshape(retained_slots, KEY_HEADS * HE...  25.5 us
    reduce_scatter x1, waiting for transfers between devices, per_device(): lax.psum_scatter(key_accumulator.reshape(retained_slots, KEY_HEADS * HEAD...  19.5 us
    unnamed x28, local copies, waits for them, and re-layouts  14.1 us
    all_gather x1, blocking collectives, per_device(): lax.all_gather(key_rotated, 'ctx', axis=0, tiled=True)  8.12 us
    dot_general x1, matrix products, per_device(): lax.dot_general(inputs, value_grad, (((0,), (0,)), ((), ())), preferred_e...  8.1 us
  transfers between devices with their start and end apart: 7, of which 5 were waited for; matrix products, arithmetic and copies ran while one was open for 9% of the time, Pallas kernels for 0%

profile of v1, /device:TPU:0, one launch (start us, length us, event | category | flops | bytes accessed | tf_op | source)
XLA Modules:
  0.0 363.7 jit_solution(12168322071289810417)
XLA Ops:
  7.2 1.2 copy.24
  8.4 2.5 collective-permute-start.1
  10.9 0.7 convert_element_type.43
  11.5 0.8 broadcast_multiply_fusion
  12.3 0.1 copy.20
  12.5 0.1 copy.21
  12.5 1.0 copy.48
  13.6 8.1 %all_gather.7 = bf16[512,512]{0,1:T(8,128)(2,1)} all-gather(bf16[128,512]{0,1:T(8,128)(2,1)S(1)} %bitcast.174), channel_id=1, replica_groups=mesh['dp'=8,'ctx'=4] {'ctx'}, dimensions={0}, use_global_device_ids=true | all-gather | bytes 655360 | tf_op jit(solution)/shard_map/all_gather | solution.py:78
  21.7 1.4 convert_bitcast_fusion
  23.2 0.4 copy.52
  23.6 0.8 subtract_convert_fusion.1
  24.4 1.4 copy.22
  25.8 1.4 copy.23
  27.2 2.1 pad_maximum_fusion
  29.3 0.9 broadcast_in_dim.72
  30.1 0.7 constant_dynamic-update-slice_fusion.3
  31.5 0.6 dynamic-slice
  32.1 0.8 dynamic-update-slice
  32.8 4.6 %all-reduce = s32[4]{0:T(128)S(1)} all-reduce(s32[4]{0:T(128)S(1)} %dynamic-update-slice), channel_id=1, replica_groups=mesh['dp'=8,'ctx'=4] {'ctx'}, use_global_device_ids=true, to_apply=%add | all-reduce | flops 4 | bytes 32
  37.5 2.0 copy.31
  39.5 2.3 copy.27
  41.8 2.3 copy.30
  44.1 0.7 constant_dynamic-update-slice_fusion.2
  44.8 0.7 constant_dynamic-update-slice_fusion.1
  45.4 3.0 collective-permute-done.2
  48.5 0.7 constant_dynamic-update-slice_fusion
  49.1 2.0 copy.29
  51.2 7.6 %while.30 = (s32[]{:T(128)}, f32[4,8,128]{2,1,0:T(8,128)S(1)}, f32[4,8,128]{2,1,0:T(8,128)S(1)}, f32[4,8,128]{2,1,0:T(8,128)S(1)}, s32[]{:T(128)}, /*index=5*/bf...) while((s32[]{:T(128)}, f32[4,8,128]{2,1,0:T(8,128)S(1)}, ...), condition=%wide.region_4.5_spmd.clone, body=%wide.region_0.4_spmd.clone.sunk | while | flops 1099120896 | bytes 35166692 | solution.py:133
  51.3 0.6 iota_compare_fusion.5
  52.0 0.2 compare_and_fusion.4
  52.2 2.3 fusion.85
  54.5 1.8 fusion.87
  56.3 2.4 fusion.86
  58.8 1.0 broadcast_in_dim.69.clone
  59.9 1.0 broadcast_in_dim.69
  60.9 1.6 broadcast_in_dim.68
  62.5 12.7 %while.31 = (s32[]{:T(128)}, f32[128,4,8,128]{3,0,2,1:T(8,128)}, f32[512,4,128]{2,0,1:T(8,128)}, f32[512,4,128]{2,0,1:T(8,128)}, s32[]{:T(128)}, /*index=5*/bf16...) while((s32[]{:T(128)}, f32[128,4,8,128]{3,0,2,1:T(8,128)}, ...), condition=%wide.region_6.7_spmd.clone, body=%wide.region_5.6_spmd.clone.sunk | while | flops 2704478464 | bytes 94034632 | solution.py:171
  62.6 0.6 iota_compare_fusion.6
  63.2 0.2 compare_and_fusion.5
  63.5 3.4 fusion.99
  66.9 1.3 fusion.102
  68.2 1.3 fusion.100
  69.5 0.3 copy-done.6
  69.8 1.5 fusion.101
  71.3 0.1 copy-done.1
  71.5 2.4 bitcast_add_fusion.2
  73.9 1.3 copy-done.2
  75.2 2.4 copy_bitcast_fusion.1
  77.7 25.5 %reduce-scatter.7.cloned.1.call-done = f32[128,512]{1,0:T(8,128)} async-done(((f32[512,512]{1,0:T(8,128)}), f32[128,512]{1,0:T(8,128)}) %reduce-scatter.7.cloned.1.call-update) | async-done | bytes 262160 | tf_op jit(solution)/shard_map/reduce_scatter | solution.py:186
  103.1 1.0 convert_element_type.49
  104.1 8.1 %convolution_bitcast_fusion.1 = f32[8192,512]{0,1:T(8,128)} fusion(bf16[128,512]{1,0:T(8,128)(2,1)S(1)} %convert_element_type.49, bf16[128,8192]{1,0:T(8,128)(2,1)S(1)} %copy-done), kind=kOutput, calls=%fused_computation.58 | convolution fusion | flops 1073741824 | bytes 19005440 | tf_op jit(solution)/shard_map/dot_general | solution.py:210
  112.3 1.1 copy-done.8
  113.5 1.3 copy.37
  114.8 0.3 reduce-scatter.11.cloned.1.call-start
  115.1 122.3 %reduce-scatter.9.cloned.1.call-done = f32[2048,512]{0,1:T(8,128)} async-done(((f32[8192,512]{0,1:T(8,128)}), f32[2048,512]{0,1:T(8,128)}) %reduce-scatter.9.cloned.1.call-update) | async-done | bytes 4194320 | tf_op jit(solution)/shard_map/reduce_scatter | solution.py:209
  237.4 0.1 copy.36
  237.5 3.0 fusion.47
  240.5 2.7 subtract_convert_fusion
  243.2 0.6 pad_maximum_fusion.1
  243.8 1.4 copy.60
  245.2 19.5 %reduce-scatter.5.cloned.1.call-done = f32[128,512]{0,1:T(8,128)} async-done(((f32[512,512]{0,1:T(8,128)}), f32[128,512]{0,1:T(8,128)}) %reduce-scatter.5.cloned.1.call-update) | async-done | bytes 262160 | tf_op jit(solution)/shard_map/reduce_scatter | solution.py:180
  264.7 1.0 subtract_convert_fusion.2
  265.7 0.8 copy.47
  266.5 90.6 %reduce-scatter.11.cloned.1.call-done = f32[2048,64]{0,1:T(8,128)} async-done(((f32[2048,512]{0,1:T(8,128)}), f32[2048,64]{0,1:T(8,128)}) %reduce-scatter.11.cloned.1.call-update) | async-done | bytes 524304 | tf_op jit(solution)/shard_map/reduce_scatter | solution.py:217
  (66 shorter events, 0.7 us)
Async XLA Ops:
  7.2 97.0 %copy-start = (bf16[128,8192]{1,0:T(8,128)(2,1)S(1)}, bf16[128,8192]{1,0:T(8,128)(2,1)}, u32[]{:S(2)}) copy-start(bf16[128,8192]{1,0:T(8,128)(2,1)} %param.17) | copy-start | bytes 6291460
  7.2 96.0 %reduce-scatter.7.cloned.1.call-start = ((), (), s32[]{:S(2)}) async-start(), calls=%async_computation.5 | async-start | bytes 1310720 | tf_op jit(solution)/shard_map/reduce_scatter | solution.py:186
  8.4 36.4 %collective-permute-start.1 = (bf16[128,512]{0,1:T(8,128)(2,1)S(1)}, bf16[128,512]{0,1:T(8,128)(2,1)S(1)}, u32[]{:S(2)}, u32[]{:S(2)}) collective-permute-start(bf16[128,512]{0,1:T(8,128)(2,1)S(1)} %copy.24), channel_id=1, source_target_pairs={{0,3},{1,0},{2,1},{3,2},{4,7},{5,4},{6,5},{7,6},{8,11},{9,8},{10,9... | collective-permute-start | bytes 393224 | tf_op jit(solution)/shard_map/ppermute | solution.py:22
  10.8 33.2 %collective-permute-start = (bf16[128,512]{0,1:T(8,128)(2,1)S(1)}, bf16[128,512]{0,1:T(8,128)(2,1)S(1)}, u32[]{:S(2)}, u32[]{:S(2)}) collective-permute-start(bf16[128,512]{0,1:T(8,128)(2,1)S(1)} %copy.24), channel_id=1, source_target_pairs={{0,1},{1,2},{2,3},{3,0},{4,5},{5,6},{6,7},{7,4},{8,9},{9,10},{10,1... | collective-permute-start | bytes 393224 | tf_op jit(solution)/shard_map/ppermute | solution.py:19
  12.3 11.2 %copy-start.16 = (f32[128,64]{0,1:T(8,128)}, f32[128,64]{0,1:T(8,128)S(1)}, u32[]{:S(2)}) copy-start(f32[128,64]{0,1:T(8,128)S(1)} %get-tuple-element.324) | copy-start | bytes 98308
  12.4 11.1 %copy-start.13 = (f32[128,64]{1,0:T(8,128)}, f32[128,64]{1,0:T(8,128)S(1)}, u32[]{:S(2)}) copy-start(f32[128,64]{1,0:T(8,128)S(1)} %copy.20) | copy-start | bytes 98308
  24.4 7.1 %copy-start.19 = (u32[32]{0:T(128)S(1)}, u32[32]{0:T(128)}, u32[]{:S(2)}) copy-start(u32[32]{0:T(128)} %constant.103) | copy-start | bytes 388
  44.1 4.4 %collective-permute-start.2 = (bf16[128,512]{0,1:T(8,128)(2,1)S(1)}, bf16[128,512]{0,1:T(8,128)(2,1)S(1)}, u32[]{:S(2)}, u32[]{:S(2)}) collective-permute-start(bf16[128,512]{0,1:T(8,128)(2,1)S(1)} %collective-permute-done), channel_id=1, source_target_pairs={{0,1},{1,2},{2,3},{3,0},{4,5},{5,6},{6,7},{7,4},{8,9},{9,10},{10,1... | collective-permute-start | bytes 393224 | tf_op jit(solution)/shard_map/ppermute | solution.py:19
  54.5 1.8 copy-start.3
  54.5 1.8 copy-start.11
  63.4 3.4 copy-start.4
  63.5 3.4 copy-start.9
  66.8 1.3 copy-start.12
  68.2 1.3 copy-start.10
  68.2 1.6 copy-start.6
  69.8 1.6 copy-start.1
  69.8 1.7 copy-start.5
  71.5 2.4 copy-start.7
  73.9 1.3 copy-start.2
  77.6 159.7 %reduce-scatter.9.cloned.1.call-start = ((), (), s32[]{:S(2)}) async-start(), calls=%async_computation.6 | async-start | bytes 20971520 | tf_op jit(solution)/shard_map/reduce_scatter | solution.py:209
  104.1 8.1 %copy-start.15 = (bf16[128,512]{1,0:T(8,128)(2,1)}, bf16[128,512]{1,0:T(8,128)(2,1)S(1)}, u32[]{:S(2)}) copy-start(bf16[128,512]{1,0:T(8,128)(2,1)S(1)} %convert_element_type.49) | copy-start | bytes 393220
  112.2 1.2 copy-start.8
  112.3 125.1 %copy-start.18 = (f32[128,64]{0,1:T(8,128)S(1)}, f32[128,64]{0,1:T(8,128)}, u32[]{:S(2)}) copy-start(f32[128,64]{0,1:T(8,128)} %get-tuple-element.322) | copy-start | bytes 98308
  112.3 152.4 %reduce-scatter.5.cloned.1.call-start = ((), (), s32[]{:S(2)}) async-start(), calls=%async_computation.4 | async-start | bytes 1310720 | tf_op jit(solution)/shard_map/reduce_scatter | solution.py:180
  114.8 242.4 %reduce-scatter.11.cloned.1.call-start = ((), (), s32[]{:S(2)}) async-start(), calls=%async_computation.7 | async-start | bytes 4718592 | tf_op jit(solution)/shard_map/reduce_scatter | solution.py:217
  237.5 3.0 copy-start.14
  243.2 21.5 %copy-start.17 = (f32[128,64]{0,1:T(8,128)S(1)}, f32[128,64]{0,1:T(8,128)}, u32[]{:S(2)}) copy-start(f32[128,64]{0,1:T(8,128)} %copy-done.16) | copy-start | bytes 98308
Sparse Core Ops, SparseCore 0:
  77.7 25.3 reduce-scatter.6
  112.4 124.9 reduce-scatter.8
  239.9 24.7 reduce-scatter.4
  268.8 88.3 reduce-scatter.10
